TPU v7x, 512 devices: a whole 4x8x8 slice. The times are simulated.
512 devices in a mesh: seq: 128 (over y, z, core), tp: 4 (over x).
Axes of the slice: x: 4, y: 8, z: 8, core: 2. Of those that a mesh axis runs over, the one named last changes fastest.
Arguments:
- tokens: bfloat16 [32768, 1280], P('seq', 'tp'), may hold values from -6 to 6
- first_gain: float32 [1280], replicated, may hold values from 0.1 to 1.9
- w_query: bfloat16 [1280, 1280], P(None, 'tp')
- w_key: bfloat16 [1280, 1280], P(None, 'tp')
- w_value: bfloat16 [1280, 1280], P(None, 'tp'), may hold values from -0.15625 to 0.15625
- w_out: bfloat16 [1280, 1280], P('tp'), may hold values from -0.625 to 0.625
- segment_ids: int32 [32768], P('seq'), may hold values from 0 to 191, never falling along the last dimension, each value on 1 to 512 neighbouring positions
- keep_mask: int32 [32768], P('seq'), may hold values 0 or 1
- merge_gain: float32 [1280], replicated, may hold values from 0.1 to 1.9
- w_merge: bfloat16 [5120, 640], P('tp'), may hold values from -0.078125 to 0.078125
- merge_index: int32 [8192, 4], P('seq'), may hold values from 0 to 32767, as said below
- destination: int32 [8192], P('seq'), may hold values from 0 to 8191, as said below
Outputs:
- delivered: bfloat16 [8192, 640], P('seq', 'tp')
Inputs may be any that keep to these rules, and one draw needn't show every extreme that they name: `segment_ids`: segment numbers never fall along the tokens; each picture or clip holds 1 to 512 tokens and one holds exactly 512. `merge_index`: the four entries of merged row m are different tokens of the device that holds row m, that is of rows (m // 64) * 256 to that plus 256 - 1; every token lies in exactly one group. `destination`: a permutation of the merged rows. The owner of row m is destination[m] // 64; the 64 rows of each device go to exactly 32 owners, exactly 2 rows to each.
All inputs are finite; a program needn't handle non-finite values. No bound on the sum of `keep_mask` on one device may be relied on, other than what follows from the above.
Results may differ from a plain program's by a relative error of at most 0.022.
Values may be sent and summed in bfloat16 or wider, within the bound.
No kernel may reach another device: no remote copies, remote signals or barrier semaphores. Data moves between devices by JAX's collectives and lax.ppermute only.
A program may use at most 64 MiB of HBM per device.

v0:
```python
import jax
import jax.numpy as jnp
from jax import lax
from jax.sharding import PartitionSpec as P

HD = 80
CAP = 2
EPS = 1e-06


def from_behind(shard, axis, by):
    length = lax.axis_size(axis)
    pairs = [(i, i + by) for i in range(length) if 0 <= i + by < length]
    return lax.ppermute(shard, axis, pairs)


def layer_norm(activations, norm_gain):
    activations = activations.astype(jnp.float32)
    row_mean = jnp.mean(activations, axis=-1, keepdims=True)
    centered = activations - row_mean
    variance = jnp.mean(centered * centered, axis=-1, keepdims=True)
    return centered * lax.rsqrt(variance + EPS) * norm_gain


def body(
    tokens,
    first_gain,
    w_query,
    w_key,
    w_value,
    w_out,
    segment_ids,
    keep_mask,
    merge_gain,
    w_merge,
    merge_index,
    destination,
):
    row_count = tokens.shape[0]
    local_width = w_query.shape[1]
    heads_here = local_width // HD
    tp_size = lax.axis_size("tp")
    seq_size = lax.axis_size("seq")
    gathered = lax.all_gather(tokens, "tp", axis=1, tiled=True)
    normed = layer_norm(gathered, first_gain).astype(jnp.bfloat16)
    queries = jnp.dot(normed, w_query, preferred_element_type=jnp.float32).astype(jnp.bfloat16)
    key_rows = jnp.dot(normed, w_key, preferred_element_type=jnp.float32).astype(jnp.bfloat16)
    value_rows = jnp.dot(normed, w_value, preferred_element_type=jnp.float32).astype(jnp.bfloat16)
    paired = jnp.concatenate([key_rows, value_rows], axis=1)
    code_query = segment_ids + 1
    code_key = jnp.where(keep_mask > 0, code_query, 0)
    pair_list = [paired]
    code_list = [code_key]
    for offset in (1, 2, -1, -2):
        moved_pair, moved_code = from_behind((paired, code_key), "seq", offset)
        pair_list.append(moved_pair)
        code_list.append(moved_code)
    all_pairs = jnp.concatenate(pair_list, axis=0)
    all_codes = jnp.concatenate(code_list, axis=0)
    window = all_pairs.shape[0]
    key_heads = all_pairs[:, :local_width].reshape(window, heads_here, HD)
    value_heads = all_pairs[:, local_width:].reshape(window, heads_here, HD)
    query_heads = queries.reshape(row_count, heads_here, HD)
    score_scale = HD ** (-0.5)
    scores = (
        jnp.einsum("qhd,khd->hqk", query_heads, key_heads, preferred_element_type=jnp.float32)
        * score_scale
    )
    query_pos = jnp.arange(row_count)[:, None]
    key_pos = jnp.arange(window)[None, :]
    allowed = (code_query[:, None] == all_codes[None, :]) | (key_pos == query_pos)
    scores = jnp.where(allowed[None], scores, -1e30)
    row_max = jnp.max(scores, axis=-1, keepdims=True)
    exponent = jnp.exp(scores - row_max)
    row_total = jnp.sum(exponent, axis=-1, keepdims=True)
    weights = (exponent / row_total).astype(jnp.bfloat16)
    attended = jnp.einsum("hqk,khd->qhd", weights, value_heads, preferred_element_type=jnp.float32)
    attended = attended.reshape(row_count, local_width).astype(jnp.bfloat16)
    position = lax.axis_index("tp")
    seq_index = lax.axis_index("seq")
    local_index = merge_index - seq_index * row_count
    order = local_index.T.reshape(row_count)
    attended_sorted = jnp.take(attended, order, axis=0)
    partial_sum = jnp.dot(attended_sorted, w_out, preferred_element_type=jnp.float32)
    mixed_sum = lax.psum_scatter(
        partial_sum.astype(jnp.bfloat16), "tp", scatter_dimension=0, tiled=True
    ).astype(jnp.float32)
    column = lax.dynamic_slice_in_dim(local_index, position, 1, 1)[:, 0]
    residual = jnp.take(gathered, column, axis=0)
    updated = residual.astype(jnp.float32) + mixed_sum
    picked = layer_norm(updated, merge_gain).astype(jnp.bfloat16)
    partial_proj = jnp.dot(picked, w_merge, preferred_element_type=jnp.float32)
    projected = lax.psum_scatter(
        partial_proj.astype(jnp.bfloat16), "tp", scatter_dimension=1, tiled=True
    )
    slot_count = projected.shape[0]
    width = projected.shape[1]
    owner = destination // slot_count
    slot = destination - owner * slot_count
    lane = jnp.arange(slot_count)
    same_owner = owner[:, None] == owner[None, :]
    earlier = lane[None, :] < lane[:, None]
    rank = jnp.sum(jnp.where(same_owner & earlier, 1, 0), axis=1)
    send_pos = owner * CAP + rank
    target = jnp.arange(seq_size * CAP)
    send_hot = (send_pos[None, :] == target[:, None]).astype(jnp.bfloat16)
    send_rows = jnp.dot(send_hot, projected, preferred_element_type=jnp.float32)
    send_rows = send_rows.astype(jnp.bfloat16).reshape(seq_size, CAP, width)
    slot_code = (slot + 1).astype(jnp.float32)
    send_slot = jnp.dot(send_hot.astype(jnp.float32), slot_code, precision=lax.Precision.HIGHEST)
    slot_row = jnp.zeros((seq_size, 1, width), jnp.bfloat16)
    slot_row = slot_row.at[:, 0, :CAP].set(send_slot.reshape(seq_size, CAP).astype(jnp.bfloat16))
    send_buf = jnp.concatenate([send_rows, slot_row], axis=1).reshape(seq_size * (CAP + 1), width)
    recv = lax.all_to_all(send_buf, "seq", 0, 0, tiled=True).reshape(seq_size, CAP + 1, width)
    recv_rows = recv[:, :CAP, :].reshape(seq_size * CAP, width)
    recv_slot = recv[:, CAP, :CAP].reshape(seq_size * CAP).astype(jnp.int32) - 1
    recv_hot = (recv_slot[None, :] == lane[:, None]).astype(jnp.bfloat16)
    delivered = jnp.dot(recv_hot, recv_rows, preferred_element_type=jnp.float32)
    return delivered.astype(jnp.bfloat16)


def solution(mesh):
    return jax.shard_map(
        body,
        mesh=mesh,
        in_specs=(
            P("seq", "tp"),
            P(),
            P(None, "tp"),
            P(None, "tp"),
            P(None, "tp"),
            P("tp", None),
            P("seq"),
            P("seq"),
            P(),
            P("tp", None),
            P("seq", None),
            P("seq"),
        ),
        out_specs=P("seq", "tp"),
        check_vma=False,
    )
```

profile of v0, /device:TPU:1, one launch (start us, length us, event | category | flops | bytes accessed | tf_op | source)
XLA Modules:
  0.0 177.3 jit_solution(7128493967322918882)
XLA Ops:
  6.5 11.7 %all_gather.3 = bf16[256,1280]{0,1:T(8,128)(2,1)S(1)} all-gather(bf16[256,320]{0,1:T(8,128)(2,1)} %param.14), channel_id=1, replica_groups=mesh['seq'=128,'tp'=4] {'tp'}, dimensions={1}, use_global_device_ids=true | all-gather | bytes 819200 | tf_op jit(solution)/shard_map/all_gather | solution.py:44
  20.1 0.9 pad_maximum_fusion
  20.9 7.4 %collective-permute-start = (bf16[256,640]{0,1:T(8,128)(2,1)}, bf16[256,640]{0,1:T(8,128)(2,1)}, u32[]{:S(2)}, u32[]{:S(2)}) collective-permute-start(bf16[256,640]{0,1:T(8,128)(2,1)} %get-tuple-element.23), channel_id=1, source_target_pairs={{0,4},{4,8},{8,12},{12,16},{16,20},{20,24},{24,28},{28,32},{32,36}... | collective-permute-start | bytes 983048 | tf_op jit(solution)/shard_map/ppermute | solution.py:14
  28.4 4.0 %collective-permute-start.1 = (bf16[256,640]{0,1:T(8,128)(2,1)}, bf16[256,640]{0,1:T(8,128)(2,1)S(1)}, u32[]{:S(2)}, u32[]{:S(2)}) collective-permute-start(bf16[256,640]{0,1:T(8,128)(2,1)} %get-tuple-element.23), channel_id=1, source_target_pairs={{0,8},{4,12},{8,16},{12,20},{16,24},{20,28},{24,32},{28,36},{32,40... | collective-permute-start | bytes 983048 | tf_op jit(solution)/shard_map/ppermute | solution.py:14
  32.4 2.3 %collective-permute-start.2 = (bf16[256,640]{0,1:T(8,128)(2,1)}, bf16[256,640]{0,1:T(8,128)(2,1)S(1)}, u32[]{:S(2)}, u32[]{:S(2)}) collective-permute-start(bf16[256,640]{0,1:T(8,128)(2,1)} %get-tuple-element.23), channel_id=1, source_target_pairs={{4,0},{8,4},{12,8},{16,12},{20,16},{24,20},{28,24},{32,28},{36,32}... | collective-permute-start | bytes 983048 | tf_op jit(solution)/shard_map/ppermute | solution.py:14
  34.7 1.3 collective-permute-start.3
  36.1 3.9 %collective-permute-start.4 = (s32[256]{0:T(256)S(1)}, s32[256]{0:T(256)S(1)}, u32[]{:S(2)}, u32[]{:S(2)}) collective-permute-start(s32[256]{0:T(256)S(1)} %get-tuple-element.20), channel_id=1, source_target_pairs={{0,4},{4,8},{8,12},{12,16},{16,20},{20,24},{24,28},{28,32},{32,36}... | collective-permute-start | bytes 3080 | tf_op jit(solution)/shard_map/ppermute | solution.py:14
  40.2 2.4 %convolution_convert_fusion.1 = bf16[256,320]{0,1:T(8,128)(2,1)} fusion(bf16[1280,320]{0,1:T(8,128)(2,1)} %param.16, bf16[256,1280]{0,1:T(8,128)(2,1)S(1)} %all_gather.3, f32[1280]{0:T(1024)S(1)} %copy-done.10, f32[256]{0:T(256)S(1)} %add_rsqrt_fusion, f32[256]{0:T(256)S(1)} %broadcast_multiply_fusion), kind=kOutput, calls=%fused_computation.23 | convolution fusion | flops 211435520 | bytes 1645568 | tf_op jit(solution)/shard_map/dot_general | solution.py:46
  42.6 4.0 %collective-permute-start.5 = (s32[256]{0:T(256)S(1)}, s32[256]{0:T(256)S(1)}, u32[]{:S(2)}, u32[]{:S(2)}) collective-permute-start(s32[256]{0:T(256)S(1)} %get-tuple-element.20), channel_id=1, source_target_pairs={{0,8},{4,12},{8,16},{12,20},{16,24},{20,28},{24,32},{28,36},{32,40... | collective-permute-start | bytes 3080 | tf_op jit(solution)/shard_map/ppermute | solution.py:14
  46.6 0.7 collective-permute-done.5
  47.3 1.9 %collective-permute-start.6 = (s32[256]{0:T(256)S(1)}, s32[256]{0:T(256)S(1)}, u32[]{:S(2)}, u32[]{:S(2)}) collective-permute-start(s32[256]{0:T(256)S(1)} %get-tuple-element.20), channel_id=1, source_target_pairs={{4,0},{8,4},{12,8},{16,12},{20,16},{24,20},{28,24},{32,28},{36,32}... | collective-permute-start | bytes 3080 | tf_op jit(solution)/shard_map/ppermute | solution.py:14
  49.2 4.0 %collective-permute-done.6 = s32[256]{0:T(256)S(1)} collective-permute-done((s32[256]{0:T(256)S(1)}, s32[256]{0:T(256)S(1)}, u32[]{:S(2)}, u32[]{:S(2)}) %collective-permute-start.6) | collective-permute-done | bytes 1056 | tf_op jit(solution)/shard_map/ppermute | solution.py:14
  53.3 1.3 collective-permute-start.7
  54.6 3.8 %collective-permute-done.7 = s32[256]{0:T(256)S(1)} collective-permute-done((s32[256]{0:T(256)S(1)}, s32[256]{0:T(256)S(1)}, u32[]{:S(2)}, u32[]{:S(2)}) %collective-permute-start.7) | collective-permute-done | bytes 1056 | tf_op jit(solution)/shard_map/ppermute | solution.py:14
  58.3 1.0 fusion.12
  59.3 1.0 constant_dynamic-update-slice_fusion.3
  60.5 1.0 fusion.54
  61.5 2.9 %exponential_reduce_fusion = f32[4,256]{1,0:T(4,128)S(1)} fusion(pred[256,1280]{1,0:T(8,128)(4,1)S(1)} %copy-done.3, bf16[256,4,80]{0,2,1:T(8,128)(2,1)} %bitcast.38, bf16[1280,4,80]{0,2,1:T(8,128)(2,1)S(1)} %bitcast.31), kind=kOutput, calls=%fused_computation.6 | convolution fusion | flops 214959360 | bytes 1314816 | tf_op jit(solution)/shard_map/sub | solution.py:74
  64.4 4.1 %fusion.13 = bf16[4,80,256]{2,1,0:T(8,128)(2,1)} fusion(bf16[1280,4,80]{0,2,1:T(8,128)(2,1)} %bitcast.33, f32[4,256]{1,0:T(4,128)S(1)} %exponential_reduce_fusion, pred[256,1280]{1,0:T(8,128)(4,1)S(1)} %copy-done.3, bf16[256,4,80]{0,2,1:T(8,128)(2,1)} %bitcast.39, bf16[1280,4,80]{0,2,1:T(8,128)(2,1)S(1)} %bitcast.32), kind=kOutput, calls=%fused_computation.22 | convolution fusion | flops 426068224 | bytes 2297856 | tf_op jit(solution)/shard_map/hqk,khd->qhd/dot_general | solution.py:77
  68.6 1.2 copy.33
  69.7 1.2 gather_fusion.1
  70.9 1.4 convolution_convert_fusion
  72.7 0.7 gather_fusion
  73.6 34.7 %reduce-scatter.5.cloned.1.call-done = bf16[64,1280]{1,0:T(8,128)(2,1)} async-done(((bf16[256,1280]{1,0:T(8,128)(2,1)}), bf16[64,1280]{1,0:T(8,128)(2,1)}) %reduce-scatter.5.cloned.1.call-update) | async-done | bytes 163856 | tf_op jit(solution)/shard_map/reduce_scatter | solution.py:85
  108.3 1.1 fusion.18
  109.5 1.2 multiply_reduce_fusion
  110.7 1.4 convolution_convert_fusion.5
  112.1 0.8 copy.36
  113.3 25.1 %reduce-scatter.7.cloned.1.call-done = bf16[160,64]{1,0:T(8,128)(2,1)} async-done(((bf16[640,64]{1,0:T(8,128)(2,1)}), bf16[160,64]{1,0:T(8,128)(2,1)}) %reduce-scatter.7.cloned.1.call-update) | async-done | bytes 20496
  138.4 1.0 convolution_convert_fusion.4
  140.0 28.9 %all_to_all.6 = bf16[128,2,240]{2,1,0:T(2,128)(2,1)S(1)} all-to-all(bf16[128,2,240]{2,1,0:T(2,128)(2,1)S(1)} %reshape.225), channel_id=1, replica_groups=mesh['seq'=128,'tp'=4] {'seq'}, dimensions={0} | all-to-all | bytes 245760 | tf_op jit(solution)/shard_map/all_to_all | solution.py:114
  169.7 0.8 convolution_convert_fusion.6
  (75 shorter events, 4.5 us)
Async XLA Ops:
  6.5 104.2 %copy-start = (bf16[1280,640]{1,0:T(8,128)(2,1)S(1)}, bf16[1280,640]{1,0:T(8,128)(2,1)}, u32[]{:S(2)}) copy-start(bf16[1280,640]{1,0:T(8,128)(2,1)} %param.23) | copy-start | bytes 4915204
  6.5 12.1 %copy-start.10 = (f32[1280]{0:T(1024)S(1)}, f32[1280]{0:T(1024)}, u32[]{:S(2)}) copy-start(f32[1280]{0:T(1024)} %param.15) | copy-start | bytes 15364
  6.5 12.1 %copy-start.8 = (bf16[1280,320]{0,1:T(8,128)(2,1)S(1)}, bf16[1280,320]{0,1:T(8,128)(2,1)}, u32[]{:S(2)}) copy-start(bf16[1280,320]{0,1:T(8,128)(2,1)} %param.17) | copy-start | bytes 2457604
  6.5 101.8 %reduce-scatter.5.cloned.1.call-start = ((), (), s32[]{:S(2)}) async-start(), calls=%async_computation.3 | async-start | bytes 819200 | tf_op jit(solution)/shard_map/reduce_scatter | solution.py:85
  18.4 1.1 copy-start.9
  19.6 16.5 %copy-start.6 = (s32[256]{0:T(256)S(1)}, s32[256]{0:T(256)}, u32[]{:S(2)}) copy-start(s32[256]{0:T(256)} %param.20) | copy-start | bytes 3076
  19.6 16.5 %copy-start.7 = (s32[256]{0:T(256)S(1)}, s32[256]{0:T(256)}, u32[]{:S(2)}) copy-start(s32[256]{0:T(256)} %param.21) | copy-start | bytes 3076
  19.6 20.4 %copy-start.5 = (s32[64,4]{0,1:T(4,128)S(1)}, s32[64,4]{0,1:T(4,128)}, u32[]{:S(2)}) copy-start(s32[64,4]{0,1:T(4,128)} %param.24) | copy-start | bytes 3076
  20.9 38.4 %collective-permute-start = (bf16[256,640]{0,1:T(8,128)(2,1)}, bf16[256,640]{0,1:T(8,128)(2,1)}, u32[]{:S(2)}, u32[]{:S(2)}) collective-permute-start(bf16[256,640]{0,1:T(8,128)(2,1)} %get-tuple-element.23), channel_id=1, source_target_pairs={{0,4},{4,8},{8,12},{12,16},{16,20},{20,24},{24,28},{28,32},{32,36}... | collective-permute-start | bytes 983048 | tf_op jit(solution)/shard_map/ppermute | solution.py:14
  28.4 31.9 %collective-permute-start.1 = (bf16[256,640]{0,1:T(8,128)(2,1)}, bf16[256,640]{0,1:T(8,128)(2,1)S(1)}, u32[]{:S(2)}, u32[]{:S(2)}) collective-permute-start(bf16[256,640]{0,1:T(8,128)(2,1)} %get-tuple-element.23), channel_id=1, source_target_pairs={{0,8},{4,12},{8,16},{12,20},{16,24},{20,28},{24,32},{28,36},{32,40... | collective-permute-start | bytes 983048 | tf_op jit(solution)/shard_map/ppermute | solution.py:14
  32.4 28.0 %collective-permute-start.2 = (bf16[256,640]{0,1:T(8,128)(2,1)}, bf16[256,640]{0,1:T(8,128)(2,1)S(1)}, u32[]{:S(2)}, u32[]{:S(2)}) collective-permute-start(bf16[256,640]{0,1:T(8,128)(2,1)} %get-tuple-element.23), channel_id=1, source_target_pairs={{4,0},{8,4},{12,8},{16,12},{20,16},{24,20},{28,24},{32,28},{36,32}... | collective-permute-start | bytes 983048 | tf_op jit(solution)/shard_map/ppermute | solution.py:14
  34.7 25.7 %collective-permute-start.3 = (bf16[256,640]{0,1:T(8,128)(2,1)}, bf16[256,640]{0,1:T(8,128)(2,1)S(1)}, u32[]{:S(2)}, u32[]{:S(2)}) collective-permute-start(bf16[256,640]{0,1:T(8,128)(2,1)} %get-tuple-element.23), channel_id=1, source_target_pairs={{8,0},{12,4},{16,8},{20,12},{24,16},{28,20},{32,24},{36,28},{40,32... | collective-permute-start | bytes 983048 | tf_op jit(solution)/shard_map/ppermute | solution.py:14
  36.1 6.5 %collective-permute-start.4 = (s32[256]{0:T(256)S(1)}, s32[256]{0:T(256)S(1)}, u32[]{:S(2)}, u32[]{:S(2)}) collective-permute-start(s32[256]{0:T(256)S(1)} %get-tuple-element.20), channel_id=1, source_target_pairs={{0,4},{4,8},{8,12},{12,16},{16,20},{20,24},{24,28},{28,32},{32,36}... | collective-permute-start | bytes 3080 | tf_op jit(solution)/shard_map/ppermute | solution.py:14
  40.2 19.2 %copy-start.1 = (bf16[1280,640]{0,1:T(8,128)(2,1)S(1)}, bf16[1280,640]{0,1:T(8,128)(2,1)}, u32[]{:S(2)}) copy-start(bf16[1280,640]{0,1:T(8,128)(2,1)} %get-tuple-element.24) | copy-start | bytes 4915204
  42.6 4.7 %collective-permute-start.5 = (s32[256]{0:T(256)S(1)}, s32[256]{0:T(256)S(1)}, u32[]{:S(2)}, u32[]{:S(2)}) collective-permute-start(s32[256]{0:T(256)S(1)} %get-tuple-element.20), channel_id=1, source_target_pairs={{0,8},{4,12},{8,16},{12,20},{16,24},{20,28},{24,32},{28,36},{32,40... | collective-permute-start | bytes 3080 | tf_op jit(solution)/shard_map/ppermute | solution.py:14
  47.3 6.0 %collective-permute-start.6 = (s32[256]{0:T(256)S(1)}, s32[256]{0:T(256)S(1)}, u32[]{:S(2)}, u32[]{:S(2)}) collective-permute-start(s32[256]{0:T(256)S(1)} %get-tuple-element.20), channel_id=1, source_target_pairs={{4,0},{8,4},{12,8},{16,12},{20,16},{24,20},{28,24},{32,28},{36,32}... | collective-permute-start | bytes 3080 | tf_op jit(solution)/shard_map/ppermute | solution.py:14
  53.3 5.1 %collective-permute-start.7 = (s32[256]{0:T(256)S(1)}, s32[256]{0:T(256)S(1)}, u32[]{:S(2)}, u32[]{:S(2)}) collective-permute-start(s32[256]{0:T(256)S(1)} %get-tuple-element.20), channel_id=1, source_target_pairs={{8,0},{12,4},{16,8},{20,12},{24,16},{28,20},{32,24},{36,28},{40,32... | collective-permute-start | bytes 3080 | tf_op jit(solution)/shard_map/ppermute | solution.py:14
  60.5 1.0 copy-start.3
  68.6 2.3 %copy-start.2 = (bf16[320,1280]{1,0:T(8,128)(2,1)S(1)}, bf16[320,1280]{1,0:T(8,128)(2,1)}, u32[]{:S(2)}) copy-start(bf16[320,1280]{1,0:T(8,128)(2,1)} %param.19) | copy-start | bytes 2457604
  72.3 1.1 copy-start.11
  72.3 38.4 %copy-start.4 = (f32[1280]{0:T(1024)S(1)}, f32[1280]{0:T(1024)}, u32[]{:S(2)}) copy-start(f32[1280]{0:T(1024)} %param.22) | copy-start | bytes 15364
  72.3 66.1 %reduce-scatter.7.cloned.1.call-start = ((), (), s32[]{:S(2)}) async-start(), calls=%async_computation.4 | async-start | bytes 204800
Sparse Core Ops, SparseCore 0:
  72.4 35.8 reduce-scatter.4
  113.0 25.2 reduce-scatter.6
where the time goes:
time: 178 us; the launch traced here: 177 us
  waiting for transfers between devices  68.4 us (38%)
  blocking collectives  40.5 us (23%)
  starting transfers between devices  26.1 us (15%)
  matrix products  15.1 us (8%)
  between operations  13.8 us (8%)
  local copies, waits for them, and re-layouts  7.86 us (4%)
  other arithmetic  5.42 us (3%)
    reduce_scatter x1, waiting for transfers between devices, body(): lax.psum_scatter(partial_sum.astype(jnp.bfloat16), 'tp', scatter_dimensio...  34.7 us
    all_to_all x1, blocking collectives, body(): lax.all_to_all(send_buf, 'seq', 0, 0, tiled=True)  28.9 us
    ppermute x8, starting transfers between devices, from_behind(): return lax.ppermute(shard, axis, pairs)  26.1 us
    unnamed x3, waiting for transfers between devices  25.1 us
    all_gather x1, blocking collectives, body(): gathered = lax.all_gather(tokens, 'tp', axis=1, tiled=True)  11.7 us
    ppermute x8, waiting for transfers between devices, from_behind(): return lax.ppermute(shard, axis, pairs)  8.52 us
    dot_general x1, matrix products, body(): jnp.einsum('hqk,khd->qhd', weights, value_heads, preferred_element_type=j...  4.14 us
  transfers between devices with their start and end apart: 10, of which 5 were waited for; matrix products, arithmetic and copies ran while one was open for 4% of the time, Pallas kernels for 0%

commit v1 on v0

--- a/solution.py
+++ b/solution.py
@@ -6,6 +6,22 @@
 HD = 80
 CAP = 2
 EPS = 1e-06
+
+
+def collect(x, axis, dim):
+    ways, here, turn = (lax.axis_size(axis), lax.axis_index(axis), x.shape[dim])
+    lengths = [n * ways if d == dim else n for d, n in enumerate(x.shape)]
+    full = lax.dynamic_update_slice_in_dim(jnp.zeros(lengths, x.dtype), x, here * turn, axis=dim)
+    going_up = going_down = x
+    for far in range(1, ways // 2 + 1):
+        going_up = lax.ppermute(going_up, axis, [(d, (d + 1) % ways) for d in range(ways)])
+        full = lax.dynamic_update_slice_in_dim(full, going_up, (here - far) % ways * turn, axis=dim)
+        if 2 * far < ways:
+            going_down = lax.ppermute(going_down, axis, [(d, (d - 1) % ways) for d in range(ways)])
+            full = lax.dynamic_update_slice_in_dim(
+                full, going_down, (here + far) % ways * turn, axis=dim
+            )
+    return full
 
 
 def from_behind(shard, axis, by):
@@ -41,7 +57,7 @@
     heads_here = local_width // HD
     tp_size = lax.axis_size("tp")
     seq_size = lax.axis_size("seq")
-    gathered = lax.all_gather(tokens, "tp", axis=1, tiled=True)
+    gathered = collect(tokens, "tp", 1)
     normed = layer_norm(gathered, first_gain).astype(jnp.bfloat16)
     queries = jnp.dot(normed, w_query, preferred_element_type=jnp.float32).astype(jnp.bfloat16)
     key_rows = jnp.dot(normed, w_key, preferred_element_type=jnp.float32).astype(jnp.bfloat16)

time: 178 us -> 181 us (1.017)
  blocking collectives: 40.5 us -> 28.9 us
  local copies, waits for them, and re-layouts: 7.86 us -> 17.9 us
  starting transfers between devices: 26.1 us -> 35 us
  waiting for transfers between devices: 68.4 us -> 63.9 us
    all_gather x1 -> x0, blocking collectives: 11.7 us -> none  [body(): gathered = lax.all_gather(tokens, 'tp', axis=1, tiled=True)]
    dynamic_update_slice x0 -> x4, local copies, waits for them, and re-layouts: none -> 10.4 us  [the longest x2 4.64 us: collect(): lax.dynamic_update_slice_in_dim(full, going_up, (here - far) % ways * tur...]
    ppermute x0 -> x3, starting transfers between devices: none -> 9.66 us  [the longest x2 6.48 us: collect(): lax.ppermute(going_up, axis, [(d, (d + 1) % ways) for d in range(ways)])]
    reduce_scatter x1, waiting for transfers between devices: 34.7 us -> 26.7 us  [body(): lax.psum_scatter(partial_sum.astype(jnp.bfloat16), 'tp', scatter_dimensio...]
    ppermute x8, waiting for transfers between devices: 8.52 us -> 11.8 us  [from_behind(): return lax.ppermute(shard, axis, pairs)]
  transfers between devices with their start and end apart: 10 -> 13, of which waited for: 5 -> 7; matrix products, arithmetic and copies ran while one was open for 4% -> 7% of each run, Pallas kernels for 0% -> 0%
where the time goes in v1:
time: 181 us; the launch traced here: 180 us
  waiting for transfers between devices  63.9 us (35%)
  starting transfers between devices  35 us (19%)
  blocking collectives  28.9 us (16%)
  local copies, waits for them, and re-layouts  17.9 us (10%)
  matrix products  15.1 us (8%)
  between operations  14 us (8%)
  other arithmetic  5.27 us (3%)
    all_to_all x1, blocking collectives, body(): lax.all_to_all(send_buf, 'seq', 0, 0, tiled=True)  28.9 us
    reduce_scatter x1, waiting for transfers between devices, body(): lax.psum_scatter(partial_sum.astype(jnp.bfloat16), 'tp', scatter_dimensio...  26.7 us
    ppermute x8, starting transfers between devices, from_behind(): return lax.ppermute(shard, axis, pairs)  25.1 us
    unnamed x3, waiting for transfers between devices  25.1 us
    ppermute x8, waiting for transfers between devices, from_behind(): return lax.ppermute(shard, axis, pairs)  11.8 us
    ppermute x2, starting transfers between devices, collect(): lax.ppermute(going_up, axis, [(d, (d + 1) % ways) for d in range(ways)])  6.48 us
    dynamic_update_slice x2, local copies, waits for them, and re-layouts, collect(): lax.dynamic_update_slice_in_dim(full, going_up, (here - far) % ways * tur...  4.64 us
    dot_general x1, matrix products, body(): jnp.einsum('hqk,khd->qhd', weights, value_heads, preferred_element_type=j...  4.14 us
  transfers between devices with their start and end apart: 13, of which 7 were waited for; matrix products, arithmetic and copies ran while one was open for 7% of the time, Pallas kernels for 0%

profile of v1, /device:TPU:1, one launch (start us, length us, event | category | flops | bytes accessed | tf_op | source)
XLA Modules:
  0.0 180.0 jit_solution(8354308909580425365)
XLA Ops:
  6.5 1.2 copy.40
  7.7 3.9 %collective-permute-start = (bf16[256,320]{1,0:T(8,128)(2,1)S(1)}, bf16[256,320]{1,0:T(8,128)(2,1)S(1)}, u32[]{:S(2)}, u32[]{:S(2)}) collective-permute-start(bf16[256,320]{1,0:T(8,128)(2,1)S(1)} %copy.40), channel_id=1, source_target_pairs={{0,1},{1,2},{2,3},{3,0},{4,5},{5,6},{6,7},{7,4},{8,9},{9,10},{10,1... | collective-permute-start | bytes 491528 | tf_op jit(solution)/shard_map/ppermute | solution.py:17
  11.7 3.2 %collective-permute-start.1 = (bf16[256,320]{1,0:T(8,128)(2,1)S(1)}, bf16[256,320]{1,0:T(8,128)(2,1)S(1)}, u32[]{:S(2)}, u32[]{:S(2)}) collective-permute-start(bf16[256,320]{1,0:T(8,128)(2,1)S(1)} %copy.40), channel_id=1, source_target_pairs={{0,3},{1,0},{2,1},{3,2},{4,7},{5,4},{6,5},{7,6},{8,11},{9,8},{10,9... | collective-permute-start | bytes 491528 | tf_op jit(solution)/shard_map/ppermute | solution.py:20
  15.6 5.3 %collective-permute-start.7 = (s32[256]{0:T(256)S(1)}, s32[256]{0:T(256)S(1)}, u32[]{:S(2)}, u32[]{:S(2)}) collective-permute-start(s32[256]{0:T(256)S(1)} %get-tuple-element.20), channel_id=1, source_target_pairs={{0,4},{4,8},{8,12},{12,16},{16,20},{20,24},{24,28},{28,32},{32,36}... | collective-permute-start | bytes 3080 | tf_op jit(solution)/shard_map/ppermute | solution.py:30
  20.9 4.0 %collective-permute-start.8 = (s32[256]{0:T(256)S(1)}, s32[256]{0:T(256)S(1)}, u32[]{:S(2)}, u32[]{:S(2)}) collective-permute-start(s32[256]{0:T(256)S(1)} %get-tuple-element.20), channel_id=1, source_target_pairs={{0,8},{4,12},{8,16},{12,20},{16,24},{20,28},{24,32},{28,36},{32,40... | collective-permute-start | bytes 3080 | tf_op jit(solution)/shard_map/ppermute | solution.py:30
  24.9 2.0 %collective-permute-start.9 = (s32[256]{0:T(256)S(1)}, s32[256]{0:T(256)S(1)}, u32[]{:S(2)}, u32[]{:S(2)}) collective-permute-start(s32[256]{0:T(256)S(1)} %get-tuple-element.20), channel_id=1, source_target_pairs={{4,0},{8,4},{12,8},{16,12},{20,16},{24,20},{28,24},{32,28},{36,32}... | collective-permute-start | bytes 3080 | tf_op jit(solution)/shard_map/ppermute | solution.py:30
  27.9 2.6 %dynamic_update_slice.12 = bf16[256,1280]{1,0:T(8,128)(2,1)S(1)} dynamic-update-slice(bf16[256,1280]{1,0:T(8,128)(2,1)S(1)} %broadcast_in_dim.47, bf16[256,320]{1,0:T(8,128)(2,1)S(1)} %copy.40, s32[]{:T(128)} %constant.116.clone.1, s32[]{:T(128)S(6)} %select_n.81) | dynamic-update-slice | bytes 327684 | tf_op jit(solution)/shard_map/dynamic_update_slice | solution.py:14
  30.5 1.3 collective-permute-start.10
  31.8 2.5 %collective-permute-start.2 = (bf16[256,320]{1,0:T(8,128)(2,1)S(1)}, bf16[256,320]{1,0:T(8,128)(2,1)S(1)}, u32[]{:S(2)}, u32[]{:S(2)}) collective-permute-start(bf16[256,320]{1,0:T(8,128)(2,1)S(1)} %collective-permute-done), channel_id=1, source_target_pairs={{0,1},{1,2},{2,3},{3,0},{4,5},{5,6},{6,7},{7,4},{8,9},{9,10},{10,1... | collective-permute-start | bytes 491528 | tf_op jit(solution)/shard_map/ppermute | solution.py:17
  34.4 1.2 collective-permute-done.10
  35.6 2.4 %dynamic_update_slice.13 = bf16[256,1280]{1,0:T(8,128)(2,1)S(1)} dynamic-update-slice(bf16[256,1280]{1,0:T(8,128)(2,1)S(1)} %dynamic_update_slice.12, bf16[256,320]{1,0:T(8,128)(2,1)S(1)} %collective-permute-done, s32[]{:T(128)} %constant.116.clone.1, s32[]{:T(128)S(6)} %select_n.83) | dynamic-update-slice | bytes 327684 | tf_op jit(solution)/shard_map/dynamic_update_slice | solution.py:18
  38.0 3.2 %dynamic_update_slice.14 = bf16[256,1280]{1,0:T(8,128)(2,1)S(1)} dynamic-update-slice(bf16[256,1280]{1,0:T(8,128)(2,1)S(1)} %dynamic_update_slice.13, bf16[256,320]{1,0:T(8,128)(2,1)S(1)} %collective-permute-done.1, s32[]{:T(128)} %constant.116.clone.1, s32[]{:T(128)S(6)} %select_n.85) | dynamic-update-slice | bytes 327684 | tf_op jit(solution)/shard_map/dynamic_update_slice | solution.py:21
  41.5 2.2 %dynamic_update_slice.15 = bf16[256,1280]{1,0:T(8,128)(2,1)S(1)} dynamic-update-slice(bf16[256,1280]{1,0:T(8,128)(2,1)S(1)} %dynamic_update_slice.14, bf16[256,320]{1,0:T(8,128)(2,1)S(1)} %collective-permute-done.2, s32[]{:T(128)} %constant.116.clone.1, s32[]{:T(128)S(6)} %select_n.87) | dynamic-update-slice | bytes 327684 | tf_op jit(solution)/shard_map/dynamic_update_slice | solution.py:18
  44.3 1.7 convolution_convert_fusion.3
  46.6 5.2 %collective-permute-start.3 = (bf16[256,640]{0,1:T(8,128)(2,1)S(1)}, bf16[256,640]{0,1:T(8,128)(2,1)S(1)}, u32[]{:S(2)}, u32[]{:S(2)}) collective-permute-start(bf16[256,640]{0,1:T(8,128)(2,1)S(1)} %get-tuple-element.23), channel_id=1, source_target_pairs={{0,4},{4,8},{8,12},{12,16},{16,20},{20,24},{24,28},{28,32},{32,36}... | collective-permute-start | bytes 983048 | tf_op jit(solution)/shard_map/ppermute | solution.py:30
  52.0 4.1 %collective-permute-start.4 = (bf16[256,640]{0,1:T(8,128)(2,1)S(1)}, bf16[256,640]{0,1:T(8,128)(2,1)S(1)}, u32[]{:S(2)}, u32[]{:S(2)}) collective-permute-start(bf16[256,640]{0,1:T(8,128)(2,1)S(1)} %get-tuple-element.23), channel_id=1, source_target_pairs={{0,8},{4,12},{8,16},{12,20},{16,24},{20,28},{24,32},{28,36},{32,40... | collective-permute-start | bytes 983048 | tf_op jit(solution)/shard_map/ppermute | solution.py:30
  56.2 1.9 %collective-permute-start.5 = (bf16[256,640]{0,1:T(8,128)(2,1)S(1)}, bf16[256,640]{0,1:T(8,128)(2,1)S(1)}, u32[]{:S(2)}, u32[]{:S(2)}) collective-permute-start(bf16[256,640]{0,1:T(8,128)(2,1)S(1)} %get-tuple-element.23), channel_id=1, source_target_pairs={{4,0},{8,4},{12,8},{16,12},{20,16},{24,20},{28,24},{32,28},{36,32}... | collective-permute-start | bytes 983048 | tf_op jit(solution)/shard_map/ppermute | solution.py:30
  58.1 1.3 collective-permute-start.6
  59.4 1.2 convolution_convert_fusion.1
  60.6 2.2 %collective-permute-done.4 = bf16[256,640]{0,1:T(8,128)(2,1)S(1)} collective-permute-done((bf16[256,640]{0,1:T(8,128)(2,1)S(1)}, bf16[256,640]{0,1:T(8,128)(2,1)S(1)}, u32[]{:S(2)}, u32[]{:S(2)}) %collective-permute-start.4) | collective-permute-done | bytes 327712 | tf_op jit(solution)/shard_map/ppermute | solution.py:30
  62.8 2.4 %collective-permute-done.5 = bf16[256,640]{0,1:T(8,128)(2,1)S(1)} collective-permute-done((bf16[256,640]{0,1:T(8,128)(2,1)S(1)}, bf16[256,640]{0,1:T(8,128)(2,1)S(1)}, u32[]{:S(2)}, u32[]{:S(2)}) %collective-permute-start.5) | collective-permute-done | bytes 327712 | tf_op jit(solution)/shard_map/ppermute | solution.py:30
  65.3 6.0 %collective-permute-done.6 = bf16[256,640]{0,1:T(8,128)(2,1)S(1)} collective-permute-done((bf16[256,640]{0,1:T(8,128)(2,1)S(1)}, bf16[256,640]{0,1:T(8,128)(2,1)S(1)}, u32[]{:S(2)}, u32[]{:S(2)}) %collective-permute-start.6) | collective-permute-done | bytes 327712 | tf_op jit(solution)/shard_map/ppermute | solution.py:30
  72.2 2.9 %exponential_reduce_fusion = f32[4,256]{1,0:T(4,128)S(1)} fusion(pred[256,1280]{1,0:T(8,128)(4,1)S(1)} %fusion.12, bf16[256,4,80]{0,2,1:T(8,128)(2,1)} %bitcast.38, bf16[1280,4,80]{0,2,1:T(8,128)(2,1)S(1)} %bitcast.31), kind=kOutput, calls=%fused_computation.6 | convolution fusion | flops 214959360 | bytes 1314816 | tf_op jit(solution)/shard_map/sub | solution.py:90
  75.2 4.1 %fusion.13 = bf16[4,80,256]{2,1,0:T(8,128)(2,1)} fusion(bf16[1280,4,80]{0,2,1:T(8,128)(2,1)} %bitcast.33, f32[4,256]{1,0:T(4,128)S(1)} %exponential_reduce_fusion, pred[256,1280]{1,0:T(8,128)(4,1)S(1)} %fusion.12, bf16[256,4,80]{0,2,1:T(8,128)(2,1)} %bitcast.39, bf16[1280,4,80]{0,2,1:T(8,128)(2,1)S(1)} %bitcast.32), kind=kOutput, calls=%fused_computation.22 | convolution fusion | flops 426068224 | bytes 2297856 | tf_op jit(solution)/shard_map/hqk,khd->qhd/dot_general | solution.py:93
  79.3 1.2 copy.43
  80.5 1.2 gather_fusion.1
  81.7 1.4 convolution_convert_fusion
  84.3 26.7 %reduce-scatter.5.cloned.1.call-done = bf16[64,1280]{1,0:T(8,128)(2,1)} async-done(((bf16[256,1280]{1,0:T(8,128)(2,1)}), bf16[64,1280]{1,0:T(8,128)(2,1)}) %reduce-scatter.5.cloned.1.call-update) | async-done | bytes 163856 | tf_op jit(solution)/shard_map/reduce_scatter | solution.py:101
  112.2 1.2 multiply_reduce_fusion
  113.4 1.4 convolution_convert_fusion.5
  116.0 25.1 %reduce-scatter.7.cloned.1.call-done = bf16[160,64]{1,0:T(8,128)(2,1)} async-done(((bf16[640,64]{1,0:T(8,128)(2,1)}), bf16[160,64]{1,0:T(8,128)(2,1)}) %reduce-scatter.7.cloned.1.call-update) | async-done | bytes 20496
  142.7 28.9 %all_to_all.6 = bf16[128,2,240]{2,1,0:T(2,128)(2,1)S(1)} all-to-all(bf16[128,2,240]{2,1,0:T(2,128)(2,1)S(1)} %reshape.225), channel_id=1, replica_groups=mesh['seq'=128,'tp'=4] {'seq'}, dimensions={0} | all-to-all | bytes 245760 | tf_op jit(solution)/shard_map/all_to_all | solution.py:130
  (77 shorter events, 11.0 us)
Async XLA Ops:
  6.5 106.9 %copy-start = (bf16[1280,640]{1,0:T(8,128)(2,1)S(1)}, bf16[1280,640]{1,0:T(8,128)(2,1)}, u32[]{:S(2)}) copy-start(bf16[1280,640]{1,0:T(8,128)(2,1)} %param.23) | copy-start | bytes 4915204
  6.5 104.5 %reduce-scatter.5.cloned.1.call-start = ((), (), s32[]{:S(2)}) async-start(), calls=%async_computation.3 | async-start | bytes 819200 | tf_op jit(solution)/shard_map/reduce_scatter | solution.py:101
  7.7 24.1 %collective-permute-start = (bf16[256,320]{1,0:T(8,128)(2,1)S(1)}, bf16[256,320]{1,0:T(8,128)(2,1)S(1)}, u32[]{:S(2)}, u32[]{:S(2)}) collective-permute-start(bf16[256,320]{1,0:T(8,128)(2,1)S(1)} %copy.40), channel_id=1, source_target_pairs={{0,1},{1,2},{2,3},{3,0},{4,5},{5,6},{6,7},{7,4},{8,9},{9,10},{10,1... | collective-permute-start | bytes 491528 | tf_op jit(solution)/shard_map/ppermute | solution.py:17
  11.7 26.3 %collective-permute-start.1 = (bf16[256,320]{1,0:T(8,128)(2,1)S(1)}, bf16[256,320]{1,0:T(8,128)(2,1)S(1)}, u32[]{:S(2)}, u32[]{:S(2)}) collective-permute-start(bf16[256,320]{1,0:T(8,128)(2,1)S(1)} %copy.40), channel_id=1, source_target_pairs={{0,3},{1,0},{2,1},{3,2},{4,7},{5,4},{6,5},{7,6},{8,11},{9,8},{10,9... | collective-permute-start | bytes 491528 | tf_op jit(solution)/shard_map/ppermute | solution.py:20
  15.6 14.9 %collective-permute-start.7 = (s32[256]{0:T(256)S(1)}, s32[256]{0:T(256)S(1)}, u32[]{:S(2)}, u32[]{:S(2)}) collective-permute-start(s32[256]{0:T(256)S(1)} %get-tuple-element.20), channel_id=1, source_target_pairs={{0,4},{4,8},{8,12},{12,16},{16,20},{20,24},{24,28},{28,32},{32,36}... | collective-permute-start | bytes 3080 | tf_op jit(solution)/shard_map/ppermute | solution.py:30
  20.9 10.9 %collective-permute-start.8 = (s32[256]{0:T(256)S(1)}, s32[256]{0:T(256)S(1)}, u32[]{:S(2)}, u32[]{:S(2)}) collective-permute-start(s32[256]{0:T(256)S(1)} %get-tuple-element.20), channel_id=1, source_target_pairs={{0,8},{4,12},{8,16},{12,20},{16,24},{20,28},{24,32},{28,36},{32,40... | collective-permute-start | bytes 3080 | tf_op jit(solution)/shard_map/ppermute | solution.py:30
  24.9 9.5 %collective-permute-start.9 = (s32[256]{0:T(256)S(1)}, s32[256]{0:T(256)S(1)}, u32[]{:S(2)}, u32[]{:S(2)}) collective-permute-start(s32[256]{0:T(256)S(1)} %get-tuple-element.20), channel_id=1, source_target_pairs={{4,0},{8,4},{12,8},{16,12},{20,16},{24,20},{28,24},{32,28},{36,32}... | collective-permute-start | bytes 3080 | tf_op jit(solution)/shard_map/ppermute | solution.py:30
  27.8 16.5 %copy-start.6 = (f32[1280]{0:T(1024)S(1)}, f32[1280]{0:T(1024)}, u32[]{:S(2)}) copy-start(f32[1280]{0:T(1024)} %param.15) | copy-start | bytes 15364
  30.5 5.2 %collective-permute-start.10 = (s32[256]{0:T(256)S(1)}, s32[256]{0:T(256)S(1)}, u32[]{:S(2)}, u32[]{:S(2)}) collective-permute-start(s32[256]{0:T(256)S(1)} %get-tuple-element.20), channel_id=1, source_target_pairs={{8,0},{12,4},{16,8},{20,12},{24,16},{28,20},{32,24},{36,28},{40,32... | collective-permute-start | bytes 3080 | tf_op jit(solution)/shard_map/ppermute | solution.py:30
  31.8 9.7 %collective-permute-start.2 = (bf16[256,320]{1,0:T(8,128)(2,1)S(1)}, bf16[256,320]{1,0:T(8,128)(2,1)S(1)}, u32[]{:S(2)}, u32[]{:S(2)}) collective-permute-start(bf16[256,320]{1,0:T(8,128)(2,1)S(1)} %collective-permute-done), channel_id=1, source_target_pairs={{0,1},{1,2},{2,3},{3,0},{4,5},{5,6},{6,7},{7,4},{8,9},{9,10},{10,1... | collective-permute-start | bytes 491528 | tf_op jit(solution)/shard_map/ppermute | solution.py:17
  43.9 2.0 %copy-start.4 = (bf16[1280,320]{0,1:T(8,128)(2,1)S(1)}, bf16[1280,320]{0,1:T(8,128)(2,1)}, u32[]{:S(2)}) copy-start(bf16[1280,320]{0,1:T(8,128)(2,1)} %param.18) | copy-start | bytes 2457604
  46.0 13.4 %copy-start.5 = (bf16[1280,320]{0,1:T(8,128)(2,1)S(1)}, bf16[1280,320]{0,1:T(8,128)(2,1)}, u32[]{:S(2)}) copy-start(bf16[1280,320]{0,1:T(8,128)(2,1)} %param.16) | copy-start | bytes 2457604
  46.6 14.0 %collective-permute-start.3 = (bf16[256,640]{0,1:T(8,128)(2,1)S(1)}, bf16[256,640]{0,1:T(8,128)(2,1)S(1)}, u32[]{:S(2)}, u32[]{:S(2)}) collective-permute-start(bf16[256,640]{0,1:T(8,128)(2,1)S(1)} %get-tuple-element.23), channel_id=1, source_target_pairs={{0,4},{4,8},{8,12},{12,16},{16,20},{20,24},{24,28},{28,32},{32,36}... | collective-permute-start | bytes 983048 | tf_op jit(solution)/shard_map/ppermute | solution.py:30
  52.0 10.8 %collective-permute-start.4 = (bf16[256,640]{0,1:T(8,128)(2,1)S(1)}, bf16[256,640]{0,1:T(8,128)(2,1)S(1)}, u32[]{:S(2)}, u32[]{:S(2)}) collective-permute-start(bf16[256,640]{0,1:T(8,128)(2,1)S(1)} %get-tuple-element.23), channel_id=1, source_target_pairs={{0,8},{4,12},{8,16},{12,20},{16,24},{20,28},{24,32},{28,36},{32,40... | collective-permute-start | bytes 983048 | tf_op jit(solution)/shard_map/ppermute | solution.py:30
  56.2 9.1 %collective-permute-start.5 = (bf16[256,640]{0,1:T(8,128)(2,1)S(1)}, bf16[256,640]{0,1:T(8,128)(2,1)S(1)}, u32[]{:S(2)}, u32[]{:S(2)}) collective-permute-start(bf16[256,640]{0,1:T(8,128)(2,1)S(1)} %get-tuple-element.23), channel_id=1, source_target_pairs={{4,0},{8,4},{12,8},{16,12},{20,16},{24,20},{28,24},{32,28},{36,32}... | collective-permute-start | bytes 983048 | tf_op jit(solution)/shard_map/ppermute | solution.py:30
  58.1 13.1 %collective-permute-start.6 = (bf16[256,640]{0,1:T(8,128)(2,1)S(1)}, bf16[256,640]{0,1:T(8,128)(2,1)S(1)}, u32[]{:S(2)}, u32[]{:S(2)}) collective-permute-start(bf16[256,640]{0,1:T(8,128)(2,1)S(1)} %get-tuple-element.23), channel_id=1, source_target_pairs={{8,0},{12,4},{16,8},{20,12},{24,16},{28,20},{32,24},{36,28},{40,32... | collective-permute-start | bytes 983048 | tf_op jit(solution)/shard_map/ppermute | solution.py:30
  79.3 2.4 %copy-start.1 = (bf16[320,1280]{1,0:T(8,128)(2,1)S(1)}, bf16[320,1280]{1,0:T(8,128)(2,1)}, u32[]{:S(2)}) copy-start(bf16[320,1280]{1,0:T(8,128)(2,1)} %param.19) | copy-start | bytes 2457604
  80.5 2.8 %copy-start.3 = (s32[64,4]{0,1:T(4,128)S(1)}, s32[64,4]{0,1:T(4,128)}, u32[]{:S(2)}) copy-start(s32[64,4]{0,1:T(4,128)} %param.24) | copy-start | bytes 3076
  80.5 2.9 %copy-start.7 = (s32[64]{0:T(128)S(1)}, s32[64]{0:T(128)}, u32[]{:S(2)}) copy-start(s32[64]{0:T(128)} %param.25) | copy-start | bytes 772
  83.1 30.4 %copy-start.2 = (f32[1280]{0:T(1024)S(1)}, f32[1280]{0:T(1024)}, u32[]{:S(2)}) copy-start(f32[1280]{0:T(1024)} %param.22) | copy-start | bytes 15364
  83.1 58.0 %reduce-scatter.7.cloned.1.call-start = ((), (), s32[]{:S(2)}) async-start(), calls=%async_computation.4 | async-start | bytes 204800
Sparse Core Ops, SparseCore 0:
  83.2 27.8 reduce-scatter.4
  115.8 25.2 reduce-scatter.6
